TPU v7x, 256 devices: a whole 4x4x8 slice. The times are simulated.
256 devices in a mesh: dp: 32 (over y, z_hi, core), tensor: 8 (over z_lo, x).
Axes of the slice: x: 4, y: 4, z: 8 (z_hi: 4, z_lo: 2; z = z_hi * 2 + z_lo), core: 2. Of those that a mesh axis runs over, the one named last changes fastest.
Arguments:
- inputs: bfloat16 [32768, 2048], P(('dp', 'tensor')), may hold values from -6 to 6
- norm_gain: float32 [2048], replicated, may hold values from 0.1 to 1.9
- proj_weight: bfloat16 [2048, 3, 2048], P('dp', None, 'tensor'), may hold values from -0.125 to 0.125
- filters: float32 [3, 7, 2048], P(None, None, 'tensor'), may hold values from -2.4 to 2.4
- cotangent: bfloat16 [32768, 2048], P('dp', 'tensor'), may hold values from -18 to 18
Outputs:
- mixed: bfloat16 [32768, 2048], P('dp', 'tensor')
- grad_inputs: bfloat16 [32768, 2048], P(('dp', 'tensor'))
- grad_proj: bfloat16 [2048, 3, 2048], P('dp', None, 'tensor')
- grad_filters: float32 [3, 7, 2048], P(None, None, 'tensor')
- grad_gain: float32 [2048], replicated
All inputs are finite; a program needn't handle non-finite values.
Results may differ from a plain program's by a relative error of at most 0.02.
Values may be sent and summed in bfloat16 or wider, within the bound.
No kernel may reach another device: no remote copies, remote signals or barrier semaphores. Data moves between devices by JAX's collectives and lax.ppermute only.
A program may use at most 64 MiB of HBM per device.

v0:
```python
import jax
import jax.numpy as jnp
from jax import lax
from jax.sharding import PartitionSpec as P


def passed_along(shard, axis, by):
    size = lax.axis_size(axis)
    pairs = [(i, i + by) for i in range(size) if 0 <= i + by < size]
    return lax.ppermute(shard, axis, pairs)


def body(inputs, norm_gain, proj_weight, filters, cotangent):
    taps = filters.shape[1]
    width = taps - 1
    wide = inputs.astype(jnp.float32)
    inv_rms = lax.rsqrt(jnp.mean(wide * wide, axis=1, keepdims=True) + 1e-05)
    normed = (wide * inv_rms * norm_gain).astype(jnp.bfloat16)
    weights = lax.all_gather(proj_weight, "dp", axis=0, tiled=True)
    positions = lax.all_gather(normed, "tensor", axis=0, tiled=True)
    length = positions.shape[0]
    streams = jnp.einsum(
        "td,dsc->tsc", positions, weights, preferred_element_type=jnp.float32
    ).astype(jnp.bfloat16)
    before = passed_along(streams[length - width :], "dp", 1)
    extended = jnp.concatenate([before, streams], axis=0).astype(jnp.float32)
    conv = jnp.zeros(streams.shape, jnp.float32)
    for tap in range(taps):
        conv = conv + filters[:, tap, :] * extended[width - tap : width - tap + length]
    mixed = (conv[:, 0] * conv[:, 1] * conv[:, 2]).astype(jnp.bfloat16)
    grad_out = cotangent.astype(jnp.float32)
    grad_conv = jnp.stack(
        [
            grad_out * conv[:, 1] * conv[:, 2],
            grad_out * conv[:, 0] * conv[:, 2],
            grad_out * conv[:, 0] * conv[:, 1],
        ],
        axis=1,
    )
    after = passed_along(grad_conv[:width], "dp", -1)
    grad_extended = jnp.concatenate([grad_conv, after], axis=0)
    grad_acc = jnp.zeros(streams.shape, jnp.float32)
    for tap in range(taps):
        grad_acc = grad_acc + filters[:, tap, :] * grad_extended[tap : tap + length]
    grad_streams = grad_acc.astype(jnp.bfloat16)
    filter_local = jnp.stack(
        [
            jnp.sum(grad_conv * extended[width - tap : width - tap + length], axis=0)
            for tap in range(taps)
        ],
        axis=1,
    )
    normed_terms = jnp.einsum(
        "tsc,dsc->td", grad_streams, weights, preferred_element_type=jnp.float32
    )
    grad_normed = lax.psum_scatter(
        normed_terms.astype(jnp.bfloat16), "tensor", scatter_dimension=0, tiled=True
    ).astype(jnp.float32)
    weight_terms = jnp.einsum(
        "td,tsc->dsc", positions, grad_streams, preferred_element_type=jnp.float32
    )
    grad_proj = lax.psum_scatter(
        weight_terms.astype(jnp.bfloat16), "dp", scatter_dimension=0, tiled=True
    )
    scaled = norm_gain * grad_normed
    grad_inputs = inv_rms * (
        scaled - wide * inv_rms * inv_rms * jnp.mean(scaled * wide, axis=1, keepdims=True)
    )
    gain_local = jnp.sum(grad_normed * wide * inv_rms, axis=0)
    grad_filters = lax.psum(filter_local, "dp")
    grad_gain = lax.psum(gain_local, ("dp", "tensor"))
    return (mixed, grad_inputs.astype(jnp.bfloat16), grad_proj, grad_filters, grad_gain)


def solution(mesh):
    return jax.shard_map(
        body,
        mesh=mesh,
        in_specs=(
            P(("dp", "tensor"), None),
            P(),
            P("dp", None, "tensor"),
            P(None, None, "tensor"),
            P("dp", "tensor"),
        ),
        out_specs=(
            P("dp", "tensor"),
            P(("dp", "tensor"), None),
            P("dp", None, "tensor"),
            P(None, None, "tensor"),
            P(),
        ),
        check_vma=False,
    )
```

profile of v0, /device:TPU:1, one launch (start us, length us, event | category | flops | bytes accessed | tf_op | source)
XLA Modules:
  0.0 393.9 jit_solution(4973453960555978686)
XLA Ops:
  7.2 0.0 all-gather.5.cloned.1.call-start
  7.2 0.7 all-gather.5.cloned.1.call-update
  7.9 0.0 all-gather.3.cloned.1.call-start
  7.9 1.2 fusion.26
  9.2 2.0 fusion.20
  11.2 0.0 all-gather.3.cloned.1.call-update
  11.2 0.0 reduce-scatter.3.cloned.1.call-start
  11.3 1.0 fusion.30
  12.3 59.7 %all-gather.5.cloned.1.call-done = bf16[2048,3,256]{2,0,1:T(8,128)(2,1)} async-done(((bf16[64,3,256]{2,0,1:T(8,128)(2,1)}), bf16[2048,3,256]{2,0,1:T(8,128)(2,1)}) %all-gather.5.cloned.1.call-update) | async-done | bytes 3145744 | tf_op jit(solution)/shard_map/all_gather | solution.py:19
  72.0 54.9 %all-gather.3.cloned.1.call-done = bf16[1024,2048]{1,0:T(8,128)(2,1)} async-done(((bf16[128,2048]{1,0:T(8,128)(2,1)}), bf16[1024,2048]{1,0:T(8,128)(2,1)}) %all-gather.3.cloned.1.call-update) | async-done | bytes 4194320 | tf_op jit(solution)/shard_map/all_gather | solution.py:20
  126.9 6.6 %fusion.14 = bf16[1024,3,256]{2,0,1:T(8,128)(2,1)S(1)} fusion(bf16[2048,3,256]{2,0,1:T(8,128)(2,1)} %all-gather.5.cloned.1.call-done, bf16[1024,2048]{1,0:T(8,128)(2,1)} %all-gather.3.cloned.1.call-done), kind=kOutput, calls=%fused_computation.33 | convolution fusion | flops 3222011904 | bytes 8912896 | tf_op jit(solution)/shard_map/td,dsc->tsc/dot_general | solution.py:22
  133.5 4.7 %collective-permute-start = (bf16[6,3,256]{2,0,1:T(8,128)(2,1)S(1)}, bf16[6,3,256]{2,0,1:T(8,128)(2,1)S(1)}, u32[]{:S(2)}, u32[]{:S(2)}) collective-permute-start(bf16[6,3,256]{2,0,1:T(8,128)(2,1)S(1)} %slice.120), channel_id=1, source_target_pairs={{0,8},{8,16},{16,24},{24,32},{32,40},{40,48},{48,56},{56,64},{64,7... | collective-permute-start | bytes 27656 | tf_op jit(solution)/shard_map/ppermute | solution.py:10
  138.3 0.8 collective-permute-done
  139.1 0.3 maximum_convert_fusion
  139.4 0.0 copy-start.1
  139.4 2.6 multiply_add_fusion
  142.0 1.2 fusion.25
  143.2 2.9 multiply_reduce_fusion
  146.0 1.9 collective-permute-start.1
  148.0 4.8 %collective-permute-done.1 = f32[6,3,256]{2,0,1:T(8,128)S(1)} collective-permute-done((f32[6,3,256]{2,0,1:T(8,128)S(1)}, f32[6,3,256]{2,0,1:T(8,128)S(1)}, u32[]{:S(2)}, u32[]{:S(2)}) %collective-permute-start.1) | collective-permute-done | bytes 18464 | tf_op jit(solution)/shard_map/ppermute | solution.py:10
  152.8 0.2 pad_maximum_fusion
  153.0 2.7 fusion.8
  155.8 5.1 %bitcast_convert_fusion = bf16[1024,2048]{1,0:T(8,128)(2,1)} fusion(bf16[1024,3,256]{2,0,1:T(8,128)(2,1)S(1)} %fusion.8, bf16[2048,3,256]{2,0,1:T(8,128)(2,1)S(1)} %copy-done.3), kind=kOutput, calls=%fused_computation | convolution fusion | flops 3223322624 | bytes 8912896 | tf_op jit(solution)/shard_map/tsc,dsc->td/dot_general | solution.py:53
  160.8 0.0 reduce-scatter.3.cloned.1.call-update
  160.9 0.2 reduce-scatter.5.cloned.1.call-start
  161.1 7.5 %fusion.4 = bf16[2048,3,256]{2,0,1:T(8,128)(2,1)} fusion(bf16[1024,3,256]{2,0,1:T(8,128)(2,1)S(1)} %fusion.8, bf16[1024,2048]{1,0:T(8,128)(2,1)} %all-gather.3.cloned.1.call-done), kind=kOutput, calls=%fused_computation.5 | convolution fusion | flops 3222798336 | bytes 8912896 | tf_op jit(solution)/shard_map/td,tsc->dsc/dot_general | solution.py:59
  168.6 0.0 reduce-scatter.5.cloned.1.call-update
  168.7 135.1 %psum.14 = f32[3,7,256]{2,0,1:T(4,128)S(1)} all-reduce(f32[3,7,256]{2,0,1:T(4,128)S(1)} %constant_dynamic-update-slice_fusion), channel_id=1, replica_groups=mesh['dp'=32,'tensor'=8] {'dp'}, use_global_device_ids=true, to_apply=%region_11.0 | all-reduce | flops 5376 | bytes 43008 | tf_op jit(solution)/shard_map/psum | solution.py:70
  303.8 0.6 copy.12
  304.5 1.4 fusion.29
  305.8 79.3 %psum.15 = f32[2048]{0:T(1024)} all-reduce(f32[2048]{0:T(1024)S(1)} %get-tuple-element.17), channel_id=1, replica_groups=mesh['dp'=32,'tensor'=8] {'dp','tensor'}, use_global_device_ids=true, to_apply=%region_13.0 | all-reduce | flops 2048 | bytes 16384 | tf_op jit(solution)/shard_map/psum | solution.py:71
  385.2 2.2 fusion.23
  (24 shorter events, 0.1 us)
Async XLA Ops:
  7.2 64.9 %all-gather.5.cloned.1.call-start = ((), (), s32[]{:S(2)}) async-start(), calls=%async_computation.3 | async-start | bytes 3244032 | tf_op jit(solution)/shard_map/all_gather | solution.py:19
  7.9 119.0 %all-gather.3.cloned.1.call-start = ((), (), s32[]{:S(2)}) async-start(), calls=%async_computation.2 | async-start | bytes 4718592 | tf_op jit(solution)/shard_map/all_gather | solution.py:20
  11.2 293.2 %reduce-scatter.3.cloned.1.call-start = ((), (), s32[]{:S(2)}) async-start(), calls=%async_computation.4 | async-start | bytes 4718592 | tf_op jit(solution)/shard_map/reduce_scatter | solution.py:56
  133.5 5.5 %collective-permute-start = (bf16[6,3,256]{2,0,1:T(8,128)(2,1)S(1)}, bf16[6,3,256]{2,0,1:T(8,128)(2,1)S(1)}, u32[]{:S(2)}, u32[]{:S(2)}) collective-permute-start(bf16[6,3,256]{2,0,1:T(8,128)(2,1)S(1)} %slice.120), channel_id=1, source_target_pairs={{0,8},{8,16},{16,24},{24,32},{32,40},{40,48},{48,56},{56,64},{64,7... | collective-permute-start | bytes 27656 | tf_op jit(solution)/shard_map/ppermute | solution.py:10
  139.4 2.6 copy-start.1
  146.0 6.8 %collective-permute-start.1 = (f32[6,3,256]{2,0,1:T(8,128)S(1)}, f32[6,3,256]{2,0,1:T(8,128)S(1)}, u32[]{:S(2)}, u32[]{:S(2)}) collective-permute-start(f32[6,3,256]{2,0,1:T(8,128)S(1)} %slice.131), channel_id=1, source_target_pairs={{8,0},{16,8},{24,16},{32,24},{40,32},{48,40},{56,48},{64,56},{72,6... | collective-permute-start | bytes 55304 | tf_op jit(solution)/shard_map/ppermute | solution.py:10
  153.0 2.7 copy-start.3
  160.9 226.5 %reduce-scatter.5.cloned.1.call-start = ((), (), s32[]{:S(2)}) async-start(), calls=%async_computation.5 | async-start | bytes 3244032 | tf_op jit(solution)/shard_map/reduce_scatter | solution.py:62
  168.6 135.8 %copy-start = (bf16[128,2048]{1,0:T(8,128)(2,1)S(1)}, bf16[128,2048]{1,0:T(8,128)(2,1)}, u32[]{:S(2)}) copy-start(bf16[128,2048]{1,0:T(8,128)(2,1)} %param.5) | copy-start | bytes 1572868
  168.6 135.8 %copy-start.2 = (f32[2048]{0:T(1024)S(1)}, f32[2048]{0:T(1024)}, u32[]{:S(2)}) copy-start(f32[2048]{0:T(1024)} %param.6) | copy-start | bytes 24580
Sparse Core Ops, SparseCore 0:
  10.7 61.3 all-gather.4
  74.4 52.5 all-gather.2
  161.0 54.1 reduce-scatter.2
  219.5 92.7 reduce-scatter.4
where the time goes:
time: 394 us
  blocking collectives  214 us (54%)
  waiting for transfers between devices  121 us (31%)
  matrix products  19.2 us (5%)
  other arithmetic  16.6 us (4%)
  between operations  13.9 us (4%)
  starting transfers between devices  6.99 us (2%)
    psum x1, blocking collectives, body(): grad_filters = lax.psum(filter_local, 'dp')  135 us
    psum x1, blocking collectives, body(): grad_gain = lax.psum(gain_local, ('dp', 'tensor'))  79.3 us
    all_gather x1, waiting for transfers between devices, body(): weights = lax.all_gather(proj_weight, 'dp', axis=0, tiled=True)  59.7 us
    all_gather x1, waiting for transfers between devices, body(): positions = lax.all_gather(normed, 'tensor', axis=0, tiled=True)  54.9 us
  transfers between devices with their start and end apart: 6, of which 4 were waited for; matrix products, arithmetic and copies ran while one was open for 4% of the time, Pallas kernels for 0%

commit v1 on v0

--- a/solution.py
+++ b/solution.py
@@ -17,7 +17,9 @@
     inv_rms = lax.rsqrt(jnp.mean(wide * wide, axis=1, keepdims=True) + 1e-05)
     normed = (wide * inv_rms * norm_gain).astype(jnp.bfloat16)
     weights = lax.all_gather(proj_weight, "dp", axis=0, tiled=True)
-    positions = lax.all_gather(normed, "tensor", axis=0, tiled=True)
+    positions = jnp.concatenate(
+        lax.all_to_all(jnp.stack([normed] * lax.axis_size("tensor")), "tensor", 0, 0), axis=0
+    )
     length = positions.shape[0]
     streams = jnp.einsum(
         "td,dsc->tsc", positions, weights, preferred_element_type=jnp.float32

time: 394 us -> 354 us (0.90)
  waiting for transfers between devices: 121 us -> 74.6 us
    all_gather x1 -> x0, waiting for transfers between devices: 54.9 us -> none  [body(): positions = lax.all_gather(normed, 'tensor', axis=0, tiled=True)]
    all_gather x1, waiting for transfers between devices: 59.7 us -> 68.6 us  [body(): weights = lax.all_gather(proj_weight, 'dp', axis=0, tiled=True)]
    all_to_all x0 -> x1, starting transfers between devices: none -> 6.33 us  [body(): lax.all_to_all(jnp.stack([normed] * lax.axis_size('tensor')), 'tensor', 0...]
  transfers between devices with their start and end apart: 6 -> 6, of which waited for: 4 -> 3; matrix products, arithmetic and copies ran while one was open for 4% -> 3% of each run, Pallas kernels for 0% -> 0%
where the time goes in v1:
time: 354 us
  blocking collectives  216 us (61%)
  waiting for transfers between devices  74.6 us (21%)
  matrix products  19.2 us (5%)
  other arithmetic  15.8 us (4%)
  between operations  13.9 us (4%)
  starting transfers between devices  10.8 us (3%)
    psum x1, blocking collectives, body(): grad_filters = lax.psum(filter_local, 'dp')  136 us
    psum x1, blocking collectives, body(): grad_gain = lax.psum(gain_local, ('dp', 'tensor'))  80.4 us
    all_gather x1, waiting for transfers between devices, body(): weights = lax.all_gather(proj_weight, 'dp', axis=0, tiled=True)  68.6 us
    dot_general x1, matrix products, body(): jnp.einsum('td,tsc->dsc', positions, grad_streams, preferred_element_type...  7.52 us
  transfers between devices with their start and end apart: 6, of which 3 were waited for; matrix products, arithmetic and copies ran while one was open for 3% of the time, Pallas kernels for 0%

profile of v1, /device:TPU:1, one launch (start us, length us, event | category | flops | bytes accessed | tf_op | source)
XLA Modules:
  0.0 354.0 jit_solution(17967622936366192106)
XLA Ops:
  7.2 1.2 fusion.16
  8.4 1.2 fusion.10
  9.6 2.5 stack.47
  12.1 6.3 %all-to-all-start = ((bf16[8,128,2048]{2,1,0:T(8,128)(2,1)}), bf16[8,128,2048]{2,1,0:T(8,128)(2,1)}, u32[]{:S(2)}, u32[]{:S(2)}) async-start(bf16[8,128,2048]{2,1,0:T(8,128)(2,1)} %stack.47), calls=%async_computation | async-start | bytes 8388608 | tf_op jit(solution)/shard_map/all_to_all | solution.py:21
  18.5 0.0 all-gather.2.cloned.1.call-start
  18.5 0.7 all-gather.2.cloned.1.call-update
  19.2 0.0 reduce-scatter.3.cloned.1.call-start
  19.3 68.6 %all-gather.2.cloned.1.call-done = bf16[2048,3,256]{2,0,1:T(8,128)(2,1)} async-done(((bf16[64,3,256]{2,0,1:T(8,128)(2,1)}), bf16[2048,3,256]{2,0,1:T(8,128)(2,1)}) %all-gather.2.cloned.1.call-update) | async-done | bytes 3145744 | tf_op jit(solution)/shard_map/all_gather | solution.py:19
  87.9 0.0 all-to-all-done
  87.9 6.6 %convolution_convert_fusion.1 = bf16[1024,3,256]{2,0,1:T(8,128)(2,1)S(1)} fusion(bf16[1024,2048,1]{1,0,2:T(8,128)(2,1)} %bitcast.1, bf16[2048,3,256]{2,0,1:T(8,128)(2,1)} %all-gather.2.cloned.1.call-done), kind=kOutput, calls=%fused_computation.29 | convolution fusion | flops 3222011904 | bytes 8912896 | tf_op jit(solution)/shard_map/td,dsc->tsc/dot_general | solution.py:24
  94.5 2.1 collective-permute-start
  96.6 0.9 collective-permute-done
  97.5 0.3 maximum_convert_fusion
  97.9 0.0 copy-start.1
  97.9 2.6 multiply_add_fusion
  100.5 1.1 fusion.15
  101.6 2.9 multiply_reduce_fusion
  104.5 2.1 collective-permute-start.1
  106.6 4.4 %collective-permute-done.1 = f32[6,3,256]{2,0,1:T(8,128)S(1)} collective-permute-done((f32[6,3,256]{2,0,1:T(8,128)S(1)}, f32[6,3,256]{2,0,1:T(8,128)S(1)}, u32[]{:S(2)}, u32[]{:S(2)}) %collective-permute-start.1) | collective-permute-done | bytes 18464 | tf_op jit(solution)/shard_map/ppermute | solution.py:10
  110.9 0.2 pad_maximum_fusion
  111.2 2.7 fusion.1
  113.9 0.0 copy-done.4
  113.9 5.1 %bitcast_convert_fusion = bf16[1024,2048]{1,0:T(8,128)(2,1)} fusion(bf16[1024,3,256]{2,0,1:T(8,128)(2,1)S(1)} %fusion.1, bf16[2048,3,256]{2,0,1:T(8,128)(2,1)S(1)} %copy-done.4), kind=kOutput, calls=%fused_computation | convolution fusion | flops 3223322624 | bytes 8912896 | tf_op jit(solution)/shard_map/tsc,dsc->td/dot_general | solution.py:55
  118.9 0.0 reduce-scatter.3.cloned.1.call-update
  119.0 0.2 reduce-scatter.5.cloned.1.call-start
  119.2 7.5 %convolution_convert_fusion = bf16[2048,3,256]{2,0,1:T(8,128)(2,1)} fusion(bf16[1024,2048,1]{1,0,2:T(8,128)(2,1)} %bitcast.1, bf16[1024,3,256]{2,0,1:T(8,128)(2,1)S(1)} %fusion.1), kind=kOutput, calls=%fused_computation.1 | convolution fusion | flops 3222798336 | bytes 8912896 | tf_op jit(solution)/shard_map/td,tsc->dsc/dot_general | solution.py:61
  126.7 0.0 reduce-scatter.5.cloned.1.call-update
  126.8 136.0 %psum.14 = f32[3,7,256]{2,0,1:T(4,128)S(1)} all-reduce(f32[3,7,256]{2,0,1:T(4,128)S(1)} %constant_dynamic-update-slice_fusion), channel_id=1, replica_groups=mesh['dp'=32,'tensor'=8] {'dp'}, use_global_device_ids=true, to_apply=%region_11.0 | all-reduce | flops 5376 | bytes 43008 | tf_op jit(solution)/shard_map/psum | solution.py:72
  262.9 0.6 copy.12
  263.5 1.4 fusion.19
  264.9 80.4 %psum.15 = f32[2048]{0:T(1024)} all-reduce(f32[2048]{0:T(1024)S(1)} %get-tuple-element.17), channel_id=1, replica_groups=mesh['dp'=32,'tensor'=8] {'dp','tensor'}, use_global_device_ids=true, to_apply=%region_13.0 | all-reduce | flops 2048 | bytes 16384 | tf_op jit(solution)/shard_map/psum | solution.py:73
  345.3 2.2 fusion.13
  (26 shorter events, 0.1 us)
Async XLA Ops:
  12.1 7.1 %copy-start.3 = (f32[3,7,256]{2,1,0:T(8,128)S(1)}, f32[3,7,256]{2,1,0:T(8,128)}, u32[]{:S(2)}) copy-start(f32[3,7,256]{2,1,0:T(8,128)} %param.8) | copy-start | bytes 64516
  12.1 75.7 %all-to-all-start = ((bf16[8,128,2048]{2,1,0:T(8,128)(2,1)}), bf16[8,128,2048]{2,1,0:T(8,128)(2,1)}, u32[]{:S(2)}, u32[]{:S(2)}) async-start(bf16[8,128,2048]{2,1,0:T(8,128)(2,1)} %stack.47), calls=%async_computation | async-start | bytes 8388608 | tf_op jit(solution)/shard_map/all_to_all | solution.py:21
  18.5 69.4 %all-gather.2.cloned.1.call-start = ((), (), s32[]{:S(2)}) async-start(), calls=%async_computation.3 | async-start | bytes 3244032 | tf_op jit(solution)/shard_map/all_gather | solution.py:19
  19.2 244.3 %reduce-scatter.3.cloned.1.call-start = ((), (), s32[]{:S(2)}) async-start(), calls=%async_computation.4 | async-start | bytes 4718592 | tf_op jit(solution)/shard_map/reduce_scatter | solution.py:58
  94.5 3.1 collective-permute-start
  97.9 2.6 copy-start.1
  104.5 6.5 %collective-permute-start.1 = (f32[6,3,256]{2,0,1:T(8,128)S(1)}, f32[6,3,256]{2,0,1:T(8,128)S(1)}, u32[]{:S(2)}, u32[]{:S(2)}) collective-permute-start(f32[6,3,256]{2,0,1:T(8,128)S(1)} %slice.131), channel_id=1, source_target_pairs={{8,0},{16,8},{24,16},{32,24},{40,32},{48,40},{56,48},{64,56},{72,6... | collective-permute-start | bytes 55304 | tf_op jit(solution)/shard_map/ppermute | solution.py:10
  111.2 2.7 copy-start.4
  119.0 228.5 %reduce-scatter.5.cloned.1.call-start = ((), (), s32[]{:S(2)}) async-start(), calls=%async_computation.5 | async-start | bytes 3244032 | tf_op jit(solution)/shard_map/reduce_scatter | solution.py:64
  126.7 136.8 %copy-start = (bf16[128,2048]{1,0:T(8,128)(2,1)S(1)}, bf16[128,2048]{1,0:T(8,128)(2,1)}, u32[]{:S(2)}) copy-start(bf16[128,2048]{1,0:T(8,128)(2,1)} %param.5) | copy-start | bytes 1572868
  126.7 136.8 %copy-start.2 = (f32[2048]{0:T(1024)S(1)}, f32[2048]{0:T(1024)}, u32[]{:S(2)}) copy-start(f32[2048]{0:T(1024)} %param.6) | copy-start | bytes 24580
Sparse Core Ops, SparseCore 0:
  22.0 65.8 all-gather.1
  119.1 57.2 reduce-scatter.2
  180.9 92.7 reduce-scatter.4
